TPU v7x, 128 devices: a whole 4x4x4 slice. The times are simulated.
128 devices in a mesh: dp: 8 (over z, core), seq: 16 (over y, x).
Axes of the slice: x: 4, y: 4, z: 4, core: 2. Of those that a mesh axis runs over, the one named last changes fastest.
Arguments:
- tokens: bfloat16 [8, 8192, 2048], P('dp', 'seq'), may hold values from -6 to 6
- input_gain: bfloat16 [2048], replicated, may hold values from 0.099609375 to 1.8984375
- qkv_weight: bfloat16 [2048, 6144], P(None, ('dp', 'seq')), may hold values from -0.125 to 0.125
- head_gain: bfloat16 [2048], replicated, may hold values from 0.099609375 to 1.8984375
- prefix_state: float32 [8, 16, 128, 128], P('dp'), may hold values from -256 to 256
Outputs:
- attended: bfloat16 [8, 8192, 2048], P('dp', 'seq')
All inputs are finite; a program needn't handle non-finite values.
Results may differ from a plain program's by a relative error of at most 0.0061.
Values may be sent and summed in bfloat16 or wider, within the bound.
No kernel may reach another device: no remote copies, remote signals or barrier semaphores. Data moves between devices by JAX's collectives and lax.ppermute only.
A program may use at most 128 MiB of HBM per device.

v0:
```python
import jax
import jax.numpy as jnp
from jax import lax
from jax.sharding import Mesh, PartitionSpec as P

D = 2048
H = 16
DH = 128
BLOCK = 512
epsilon = 1e-05


def feature_map(inputs):
    return jnp.where(inputs > 0, inputs + 1.0, jnp.exp(jnp.minimum(inputs, 0.0)))


def body(tokens, input_gain, qkv_weight, head_gain, prefix_state):
    inputs = tokens[0].astype(jnp.float32)
    normed = inputs * lax.rsqrt(jnp.mean(inputs * inputs, axis=-1, keepdims=True) + epsilon)
    normed = (normed * input_gain.astype(jnp.float32)).astype(jnp.bfloat16)
    tok_rows = normed.shape[0]
    weight = lax.all_gather(qkv_weight, ("dp", "y", "x"), axis=1, tiled=True)
    keys_t = lax.dot_general(
        weight[:, D : 2 * D], normed, (((0,), (1,)), ((), ())), preferred_element_type=jnp.float32
    )
    keys_t = feature_map(keys_t).astype(jnp.bfloat16).reshape(H, DH, tok_rows)
    values = jnp.dot(normed, weight[:, 2 * D :], preferred_element_type=jnp.float32)
    values = values.astype(jnp.bfloat16).reshape(tok_rows, H, DH)
    local = jnp.einsum("hdt,the->hde", keys_t, values, preferred_element_type=jnp.float32).astype(
        jnp.bfloat16
    )
    gathered = lax.all_gather(local[None], ("y", "x"), axis=0, tiled=True)
    seq_here = lax.axis_index(("y", "x"))
    earlier = (jnp.arange(gathered.shape[0]) < seq_here).astype(jnp.bfloat16)
    before = jnp.einsum("c,chde->hde", earlier, gathered, preferred_element_type=jnp.float32)
    memory = prefix_state[0] + before
    queries = jnp.dot(normed, weight[:, :D], preferred_element_type=jnp.float32)
    queries = feature_map(queries).astype(jnp.bfloat16).reshape(tok_rows, H, DH)
    causal = jnp.arange(tok_rows)[:, None] >= jnp.arange(tok_rows)[None, :]
    gains = head_gain.astype(jnp.float32).reshape(H, DH)
    scores = jnp.einsum("bhd,hdc->hbc", queries, keys_t, preferred_element_type=jnp.float32)
    scores = jnp.where(causal[None], scores, 0.0).astype(jnp.bfloat16)
    within = jnp.einsum("hbc,che->bhe", scores, values, preferred_element_type=jnp.float32)
    carried = jnp.einsum(
        "bhd,hde->bhe", queries, memory.astype(jnp.bfloat16), preferred_element_type=jnp.float32
    )
    numerator = carried + within
    scale = lax.rsqrt(jnp.mean(numerator * numerator, axis=-1, keepdims=True) + epsilon)
    attended = (numerator * scale * gains).astype(jnp.bfloat16)
    return attended.reshape(1, tok_rows, H * DH)


def solution(mesh):
    n_dp, n_seq = mesh.devices.shape
    n_x = int(round(n_seq**0.5))
    split = Mesh(mesh.devices.reshape(n_dp, n_seq // n_x, n_x), ("dp", "y", "x"))
    cols = ("y", "x")
    placed = (P("dp", cols, None), P(), P(None, ("dp", "y", "x")), P(), P("dp", None, None, None))
    return jax.shard_map(
        body, mesh=split, in_specs=placed, out_specs=P("dp", cols, None), check_vma=False
    )
```

profile of v0, /device:TPU:1, one launch (start us, length us, event | category | flops | bytes accessed | tf_op | source)
XLA Modules:
  0.0 226.6 jit_solution(10848702317231720216)
XLA Ops:
  6.5 0.0 all-gather.4.cloned.1.call-start
  6.5 0.7 all-gather.4.cloned.1.call-update
  7.3 0.0 all-gather.6.cloned.1.call-start
  7.3 0.7 convert_element_type.40
  8.0 2.1 fusion.8
  10.1 97.0 %all-gather.4.cloned.1.call-done = bf16[2048,6144]{0,1:T(8,128)(2,1)} async-done(((bf16[2048,48]{0,1:T(8,128)(2,1)}), bf16[2048,6144]{0,1:T(8,128)(2,1)}) %all-gather.4.cloned.1.call-update) | async-done | bytes 25165840 | tf_op jit(solution)/shard_map/all_gather | solution.py:22
  107.1 9.9 %fusion.14 = bf16[512,2048]{1,0:T(8,128)(2,1)} fusion(bf16[2048,6144]{0,1:T(8,128)(2,1)} %all-gather.4.cloned.1.call-done, bf16[1,512,2048]{2,1,0:T(8,128)(2,1)} %param.5, f32[2048]{0:T(1024)S(1)} %convert_element_type.40, f32[512]{0:T(512)S(1)} %add_rsqrt_fusion.1), kind=kOutput, calls=%fused_computation.21 | convolution fusion | flops 4300210176 | bytes 12593152 | tf_op jit(solution)/shard_map/dot_general | solution.py:27
  117.0 2.9 %copy.23 = bf16[512,2048]{0,1:T(8,128)(2,1)S(1)} copy(bf16[512,2048]{1,0:T(8,128)(2,1)} %fusion.14) | data formatting | bytes 4194304 | tf_op jit(solution)/shard_map/reshape | solution.py:28
  119.9 10.3 %fusion.21 = bf16[2048,512]{0,1:T(8,128)(2,1)} fusion(bf16[2048,6144]{0,1:T(8,128)(2,1)} %all-gather.4.cloned.1.call-done, bf16[1,512,2048]{2,1,0:T(8,128)(2,1)} %param.5, f32[2048]{0:T(1024)S(1)} %convert_element_type.40, f32[512]{0:T(512)S(1)} %add_rsqrt_fusion.1), kind=kOutput, calls=%fused_computation.22 | convolution fusion | flops 4304404480 | bytes 12593152 | tf_op jit(solution)/shard_map/dot_general | solution.py:23
  130.1 0.0 copy-start.3
  130.1 3.9 %copy.22 = bf16[2048,512]{1,0:T(8,128)(2,1)} copy(bf16[2048,512]{0,1:T(8,128)(2,1)} %fusion.21) | data formatting | bytes 4194304 | tf_op jit(solution)/shard_map/reshape | solution.py:26
  134.1 3.1 %convolution_convert_fusion = bf16[16,128,128]{2,1,0:T(8,128)(2,1)} fusion(bf16[16,128,512]{2,1,0:T(8,128)(2,1)} %bitcast.56, bf16[512,16,128]{0,2,1:T(8,128)(2,1)S(1)} %bitcast.54), kind=kOutput, calls=%fused_computation.30 | convolution fusion | flops 268697600 | bytes 4718592 | tf_op jit(solution)/shard_map/hdt,the->hde/dot_general | solution.py:29
  137.2 0.0 all-gather.6.cloned.1.call-update
  137.2 0.1 iota_compare_fusion
  137.3 0.0 copy-done.3
  137.3 10.4 %fusion.31 = bf16[64,16,8,128]{3,2,1,0:T(8,128)(2,1)} fusion(bf16[2048,6144]{0,1:T(8,128)(2,1)} %all-gather.4.cloned.1.call-done, bf16[1,512,2048]{2,1,0:T(8,128)(2,1)} %param.5, f32[2048]{0:T(1024)S(1)} %convert_element_type.40, f32[512]{0:T(512)S(1)} %add_rsqrt_fusion.1), kind=kOutput, calls=%fused_computation.29 | convolution fusion | flops 4304404480 | bytes 12593152 | tf_op jit(solution)/shard_map/dot_general | solution.py:37
  147.7 9.2 %fusion.24 = f32[16,128,512]{2,1,0:T(8,128)} fusion(bf16[512,16,128]{0,2,1:T(8,128)(2,1)S(1)} %bitcast.55, bf16[16,128,512]{2,1,0:T(8,128)(2,1)} %bitcast.57, pred[512,512]{1,0:T(8,128)(4,1)S(1)} %iota_compare_fusion, bf16[64,16,8,128]{3,2,1,0:T(8,128)(2,1)} %fusion.31), kind=kOutput, calls=%fused_computation.23 | convolution fusion | flops 2155872256 | bytes 10747904 | tf_op jit(solution)/shard_map/hbc,che->bhe/dot_general | solution.py:43
  156.8 50.2 %all-gather.6.cloned.1.call-done = bf16[256,128,128]{2,1,0:T(8,128)(2,1)} async-done(((bf16[16,128,128]{2,1,0:T(8,128)(2,1)}), bf16[256,128,128]{2,1,0:T(8,128)(2,1)}) %all-gather.6.cloned.1.call-update) | async-done | bytes 8388624 | tf_op jit(solution)/shard_map/all_gather | solution.py:32
  207.0 0.0 copy-start
  207.0 0.0 copy-start.1
  207.0 0.0 copy-start.2
  207.0 8.7 %fusion.6 = f32[1,16,128,128]{3,0,2,1:T(1,128)S(1)} fusion(bf16[16,16,128,128]{3,2,1,0:T(8,128)(2,1)} %bitcast.53, s32[]{:T(128)S(6)} %add.45), kind=kOutput, calls=%fused_computation.7 | convolution fusion | flops 8388624 | bytes 9437188 | tf_op jit(solution)/shard_map/c,chde->hde/dot_general | solution.py:35
  215.7 0.0 copy-done
  215.7 0.0 copy-done.1
  215.7 0.0 copy-done.2
  215.7 1.0 fusion.11
  216.8 0.6 fusion.13
  217.4 2.4 %copy.17 = bf16[1,512,2048]{2,1,0:T(8,128)(2,1)} copy(bf16[1,512,2048]{1,2,0:T(8,128)(2,1)S(1)} %bitcast.58) | data formatting | bytes 4194304 | tf_op jit(solution)/shard_map/reshape | solution.py:50
  (3 shorter events, 0.0 us)
Async XLA Ops:
  6.5 100.6 %all-gather.4.cloned.1.call-start = ((), (), s32[]{:S(2)}) async-start(), calls=%async_computation | async-start | bytes 25362432 | tf_op jit(solution)/shard_map/all_gather | solution.py:22
  7.3 199.8 %all-gather.6.cloned.1.call-start = ((), (), s32[]{:S(2)}) async-start(), calls=%async_computation.1 | async-start | bytes 8912896 | tf_op jit(solution)/shard_map/all_gather | solution.py:32
  130.1 7.2 %copy-start.3 = (bf16[2048]{0:T(1024)(128)(2,1)S(1)}, bf16[2048]{0:T(1024)(128)(2,1)}, u32[]{:S(2)}) copy-start(bf16[2048]{0:T(1024)(128)(2,1)} %param.8) | copy-start | bytes 12292
  207.0 8.7 %copy-start = (f32[16,128,512]{2,1,0:T(8,128)S(1)}, f32[16,128,512]{2,1,0:T(8,128)}, u32[]{:S(2)}) copy-start(f32[16,128,512]{2,1,0:T(8,128)} %fusion.24) | copy-start | bytes 12582916
  207.0 8.7 %copy-start.1 = (bf16[64,16,8,128]{3,2,1,0:T(8,128)(2,1)S(1)}, bf16[64,16,8,128]{3,2,1,0:T(8,128)(2,1)}, u32[]{:S(2)}) copy-start(bf16[64,16,8,128]{3,2,1,0:T(8,128)(2,1)} %fusion.31) | copy-start | bytes 6291460
  207.0 8.7 %copy-start.2 = (f32[1,16,128,128]{3,2,1,0:T(8,128)S(1)}, f32[1,16,128,128]{3,2,1,0:T(8,128)}, u32[]{:S(2)}) copy-start(f32[1,16,128,128]{3,2,1,0:T(8,128)} %param.9) | copy-start | bytes 3145732
Sparse Core Ops, SparseCore 0:
  10.4 96.6 all-gather.3
  137.3 69.6 all-gather.5
where the time goes:
time: 227 us
  waiting for transfers between devices  148 us (65%)
  matrix products  52.5 us (23%)
  between operations  13.5 us (6%)
  local copies, waits for them, and re-layouts  9.18 us (4%)
  other arithmetic  3.51 us (2%)
    all_gather x1, waiting for transfers between devices, body(): weight = lax.all_gather(qkv_weight, ('dp', 'y', 'x'), axis=1, tiled=True)  97 us
    all_gather x1, waiting for transfers between devices, body(): gathered = lax.all_gather(local[None], ('y', 'x'), axis=0, tiled=True)  50.2 us
    dot_general x1, matrix products, body(): queries = jnp.dot(normed, weight[:, :D], preferred_element_type=jnp.float32)  10.4 us
    dot_general x1, matrix products, body(): lax.dot_general(weight[:, D:2 * D], normed, (((0,), (1,)), ((), ())), pre...  10.3 us
    dot_general x1, matrix products, body(): jnp.dot(normed, weight[:, 2 * D:], preferred_element_type=jnp.float32)  9.89 us
    dot_general x1, matrix products, body(): jnp.einsum('hbc,che->bhe', scores, values, preferred_element_type=jnp.flo...  9.16 us
    dot_general x1, matrix products, body(): jnp.einsum('c,chde->hde', earlier, gathered, preferred_element_type=jnp.f...  8.66 us
  transfers between devices with their start and end apart: 2, of which 2 were waited for; matrix products, arithmetic and copies ran while one was open for 10% of the time, Pallas kernels for 0%

commit v1 on v0

--- a/solution.py
+++ b/solution.py
@@ -19,7 +19,8 @@
     normed = inputs * lax.rsqrt(jnp.mean(inputs * inputs, axis=-1, keepdims=True) + epsilon)
     normed = (normed * input_gain.astype(jnp.float32)).astype(jnp.bfloat16)
     tok_rows = normed.shape[0]
-    weight = lax.all_gather(qkv_weight, ("dp", "y", "x"), axis=1, tiled=True)
+    repeated = jnp.stack([qkv_weight] * lax.axis_size(("dp", "y", "x")))
+    weight = jnp.concatenate(lax.all_to_all(repeated, ("dp", "y", "x"), 0, 0), axis=1)
     keys_t = lax.dot_general(
         weight[:, D : 2 * D], normed, (((0,), (1,)), ((), ())), preferred_element_type=jnp.float32
     )

time: 227 us -> 556 us (2.45)
  waiting for transfers between devices: 148 us -> 459 us
  starting transfers between devices: 0.04 us -> 11.9 us
  local copies, waits for them, and re-layouts: 9.18 us -> 18.5 us
    all_to_all x0 -> x1, waiting for transfers between devices: none -> 376 us  [body(): lax.all_to_all(repeated, ('dp', 'y', 'x'), 0, 0)]
    all_gather x1 -> x0, waiting for transfers between devices: 97 us -> none  [body(): weight = lax.all_gather(qkv_weight, ('dp', 'y', 'x'), axis=1, tiled=True)]
    all_gather x1, waiting for transfers between devices: 50.2 us -> 83.4 us  [body(): gathered = lax.all_gather(local[None], ('y', 'x'), axis=0, tiled=True)]
    all_to_all x0 -> x1, starting transfers between devices: none -> 11.9 us  [body(): lax.all_to_all(repeated, ('dp', 'y', 'x'), 0, 0)]
    another operation x0 -> x1, local copies, waits for them, and re-layouts: none -> 9.34 us  [body(): repeated = jnp.stack([qkv_weight] * lax.axis_size(('dp', 'y', 'x')))]
  transfers between devices with their start and end apart: 2 -> 2, of which waited for: 2 -> 2; matrix products, arithmetic and copies ran while one was open for 10% -> 4% of each run, Pallas kernels for 0% -> 0%
where the time goes in v1:
time: 556 us
  waiting for transfers between devices  459 us (83%)
  matrix products  51.2 us (9%)
  local copies, waits for them, and re-layouts  18.5 us (3%)
  between operations  13.5 us (2%)
  starting transfers between devices  11.9 us (2%)
    all_to_all x1, waiting for transfers between devices, body(): lax.all_to_all(repeated, ('dp', 'y', 'x'), 0, 0)  376 us
    all_gather x1, waiting for transfers between devices, body(): gathered = lax.all_gather(local[None], ('y', 'x'), axis=0, tiled=True)  83.4 us
    all_to_all x1, starting transfers between devices, body(): lax.all_to_all(repeated, ('dp', 'y', 'x'), 0, 0)  11.9 us
  transfers between devices with their start and end apart: 2, of which 2 were waited for; matrix products, arithmetic and copies ran while one was open for 4% of the time, Pallas kernels for 0%

profile of v1, /device:TPU:1, one launch (start us, length us, event | category | flops | bytes accessed | tf_op | source)
XLA Modules:
  0.0 555.6 jit_solution(6321737969137162657)
XLA Ops:
  6.5 9.3 %stack.2 = bf16[128,2048,48]{1,2,0:T(8,128)(2,1)} broadcast(bf16[2048,48]{0,1:T(8,128)(2,1)} %param.7), dimensions={1,2} | broadcast | bytes 25362432 | tf_op jit(solution)/shard_map/stack | solution.py:22
  15.9 0.0 copy-start.4
  15.9 0.0 copy-start.1
  15.9 11.9 %all-to-all-start = ((bf16[128,2048,48]{1,2,0:T(8,128)(2,1)}), bf16[128,2048,48]{1,2,0:T(8,128)(2,1)}, u32[]{:S(2)}, u32[]{:S(2)}) async-start(bf16[128,2048,48]{1,2,0:T(8,128)(2,1)} %stack.2), calls=%async_computation | async-start | bytes 50331648 | tf_op jit(solution)/shard_map/all_to_all | solution.py:23
  27.8 0.0 all-gather.3.cloned.1.call-start
  27.8 0.0 copy-done.4
  27.9 0.0 copy-done.1
  27.9 0.5 fusion.8
  28.4 375.7 %all-to-all-done = bf16[128,2048,48]{1,2,0:T(8,128)(2,1)} async-done(((bf16[128,2048,48]{1,2,0:T(8,128)(2,1)}), bf16[128,2048,48]{1,2,0:T(8,128)(2,1)}, u32[]{:S(2)}, u32[]{:S(2)}) %all-to-all-start) | async-done | bytes 25165856 | tf_op jit(solution)/shard_map/all_to_all | solution.py:23
  404.0 9.7 %fusion.21 = bf16[2048,512]{0,1:T(8,128)(2,1)} fusion(bf16[2048,6144]{0,1:T(8,128)(2,1)} %bitcast.6, bf16[1,512,2048]{2,1,0:T(8,128)(2,1)S(1)} %copy-done.1, f32[2048]{0:T(1024)S(1)} %convert_element_type.40, f32[512]{0:T(512)S(1)} %add_rsqrt_fusion.1), kind=kOutput, calls=%fused_computation.22 | convolution fusion | flops 4304404480 | bytes 12593152 | tf_op jit(solution)/shard_map/dot_general | solution.py:24
  413.7 9.2 %fusion.14 = bf16[512,2048]{1,0:T(8,128)(2,1)} fusion(bf16[2048,6144]{0,1:T(8,128)(2,1)} %bitcast.6, bf16[1,512,2048]{2,1,0:T(8,128)(2,1)S(1)} %copy-done.1, f32[2048]{0:T(1024)S(1)} %convert_element_type.40, f32[512]{0:T(512)S(1)} %add_rsqrt_fusion.1), kind=kOutput, calls=%fused_computation.21 | convolution fusion | flops 4300210176 | bytes 12593152 | tf_op jit(solution)/shard_map/dot_general | solution.py:28
  422.9 2.9 copy.31
  425.8 0.0 copy-start.5
  425.8 3.9 copy.32
  429.7 3.1 convolution_convert_fusion
  432.8 0.0 all-gather.3.cloned.1.call-update
  432.8 0.1 iota_compare_fusion
  432.9 0.0 copy-done.5
  432.9 10.4 %fusion.31 = bf16[64,16,8,128]{3,2,1,0:T(8,128)(2,1)} fusion(bf16[2048,6144]{0,1:T(8,128)(2,1)} %bitcast.6, bf16[1,512,2048]{2,1,0:T(8,128)(2,1)} %param.5, f32[2048]{0:T(1024)S(1)} %convert_element_type.40, f32[512]{0:T(512)S(1)} %add_rsqrt_fusion.1), kind=kOutput, calls=%fused_computation.29 | convolution fusion | flops 4304404480 | bytes 12593152 | tf_op jit(solution)/shard_map/dot_general | solution.py:38
  443.3 9.2 %fusion.24 = f32[16,128,512]{2,1,0:T(8,128)} fusion(bf16[512,16,128]{0,2,1:T(8,128)(2,1)} %bitcast.60, bf16[16,128,512]{2,1,0:T(8,128)(2,1)S(1)} %bitcast.58, pred[512,512]{1,0:T(8,128)(4,1)S(1)} %iota_compare_fusion, bf16[64,16,8,128]{3,2,1,0:T(8,128)(2,1)} %fusion.31), kind=kOutput, calls=%fused_computation.23 | convolution fusion | flops 2155872256 | bytes 10747904 | tf_op jit(solution)/shard_map/hbc,che->bhe/dot_general | solution.py:44
  452.5 83.4 %all-gather.3.cloned.1.call-done = bf16[256,128,128]{2,1,0:T(8,128)(2,1)} async-done(((bf16[16,128,128]{2,1,0:T(8,128)(2,1)}), bf16[256,128,128]{2,1,0:T(8,128)(2,1)}) %all-gather.3.cloned.1.call-update) | async-done | bytes 8388624 | tf_op jit(solution)/shard_map/all_gather | solution.py:33
  536.0 0.0 copy-start
  536.0 0.0 copy-start.2
  536.0 0.0 copy-start.3
  536.0 8.7 %fusion.6 = f32[1,16,128,128]{3,0,2,1:T(1,128)S(1)} fusion(bf16[16,16,128,128]{3,2,1,0:T(8,128)(2,1)} %bitcast.56, s32[]{:T(128)S(6)} %add.45), kind=kOutput, calls=%fused_computation.7 | convolution fusion | flops 8388624 | bytes 9437188 | tf_op jit(solution)/shard_map/c,chde->hde/dot_general | solution.py:36
  544.6 0.0 copy-done
  544.6 0.0 copy-done.2
  544.6 0.0 copy-done.3
  544.7 1.0 fusion.11
  545.7 0.6 fusion.13
  546.3 2.4 copy.26
  (4 shorter events, 0.0 us)
Async XLA Ops:
  15.9 12.0 %copy-start.4 = (bf16[2048]{0:T(1024)(128)(2,1)S(1)}, bf16[2048]{0:T(1024)(128)(2,1)}, u32[]{:S(2)}) copy-start(bf16[2048]{0:T(1024)(128)(2,1)} %param.6) | copy-start | bytes 12292
  15.9 12.0 %copy-start.1 = (bf16[1,512,2048]{2,1,0:T(8,128)(2,1)S(1)}, bf16[1,512,2048]{2,1,0:T(8,128)(2,1)}, u32[]{:S(2)}) copy-start(bf16[1,512,2048]{2,1,0:T(8,128)(2,1)} %param.5) | copy-start | bytes 6291460
  15.9 388.1 %all-to-all-start = ((bf16[128,2048,48]{1,2,0:T(8,128)(2,1)}), bf16[128,2048,48]{1,2,0:T(8,128)(2,1)}, u32[]{:S(2)}, u32[]{:S(2)}) async-start(bf16[128,2048,48]{1,2,0:T(8,128)(2,1)} %stack.2), calls=%async_computation | async-start | bytes 50331648 | tf_op jit(solution)/shard_map/all_to_all | solution.py:23
  27.8 508.2 %all-gather.3.cloned.1.call-start = ((), (), s32[]{:S(2)}) async-start(), calls=%async_computation.1 | async-start | bytes 8912896 | tf_op jit(solution)/shard_map/all_gather | solution.py:33
  425.8 7.2 %copy-start.5 = (bf16[2048]{0:T(1024)(128)(2,1)S(1)}, bf16[2048]{0:T(1024)(128)(2,1)}, u32[]{:S(2)}) copy-start(bf16[2048]{0:T(1024)(128)(2,1)} %param.8) | copy-start | bytes 12292
  536.0 8.7 %copy-start = (f32[16,128,512]{2,1,0:T(8,128)S(1)}, f32[16,128,512]{2,1,0:T(8,128)}, u32[]{:S(2)}) copy-start(f32[16,128,512]{2,1,0:T(8,128)} %fusion.24) | copy-start | bytes 12582916
  536.0 8.7 %copy-start.2 = (bf16[64,16,8,128]{3,2,1,0:T(8,128)(2,1)S(1)}, bf16[64,16,8,128]{3,2,1,0:T(8,128)(2,1)}, u32[]{:S(2)}) copy-start(bf16[64,16,8,128]{3,2,1,0:T(8,128)(2,1)} %fusion.31) | copy-start | bytes 6291460
  536.0 8.7 %copy-start.3 = (f32[1,16,128,128]{3,2,1,0:T(8,128)S(1)}, f32[1,16,128,128]{3,2,1,0:T(8,128)}, u32[]{:S(2)}) copy-start(f32[1,16,128,128]{3,2,1,0:T(8,128)} %param.9) | copy-start | bytes 3145732
Sparse Core Ops, SparseCore 0:
  433.0 102.9 all-gather.2
